TPU v7x, 256 devices: a whole 4x4x8 slice. The times are simulated.
256 devices in a mesh: row: 16 (over z, core), col: 16 (over y, x).
Axes of the slice: x: 4, y: 4, z: 8, core: 2. Of those that a mesh axis runs over, the one named last changes fastest.
Arguments:
- matrix: bfloat16 [4096, 262144], P('row', 'col'), may hold values from -60 to 60
- test_matrix: bfloat16 [262144, 512], P(('col', 'row')), may hold values from -0.0390625 to 0.0390625
Outputs:
- orthonormal: float32 [4096, 512], P(('row', 'col'))
- triangular: float32 [512, 512], replicated
All inputs are finite; a program needn't handle non-finite values.
Results may differ from a plain program's by a relative error of at most 0.0003.
Values may be sent and summed in bfloat16 or wider, within the bound.
No kernel may reach another device: no remote copies, remote signals or barrier semaphores. Data moves between devices by JAX's collectives and lax.ppermute only.
A program may use at most 128 MiB of HBM per device.

v0:
```python
import jax
import jax.numpy as jnp
from jax import lax
from jax.sharding import PartitionSpec as P


def probe_product(matrix, test_matrix):
    return jnp.dot(
        matrix,
        lax.all_gather(test_matrix, "row", axis=0, tiled=True),
        preferred_element_type=jnp.float32,
    )


def gram_term(own_rows):
    return jnp.dot(own_rows.T, own_rows, precision=lax.Precision.HIGHEST)


def shards(matrix, test_matrix):
    share_rows = matrix.shape[0] // lax.axis_size("col")
    total_rows = matrix.shape[0] * lax.axis_size("row")
    partial_value = probe_product(matrix, test_matrix)
    sketch = lax.psum(partial_value, "col")
    gram = lax.psum(gram_term(sketch), "row")
    own_rows = lax.dynamic_slice_in_dim(sketch, lax.axis_index("col") * share_rows, share_rows, 0)
    gram = gram / jnp.float32(total_rows)
    lower_factor = jnp.linalg.cholesky(gram)
    orthonormal = lax.linalg.triangular_solve(
        lower_factor, own_rows, left_side=False, lower=True, transpose_a=True
    )
    return (orthonormal, lower_factor.T)


def solution(mesh):
    in_specs = (P("row", "col"), P(("col", "row"), None))
    out_specs = (P(("row", "col"), None), P())
    return jax.shard_map(shards, mesh=mesh, in_specs=in_specs, out_specs=out_specs, check_vma=False)
```

profile of v0, /device:TPU:1, one launch (start us, length us, event | category | flops | bytes accessed | tf_op | source)
XLA Modules:
  0.0 478.8 jit_solution(10044351522613762331)
XLA Ops:
  7.2 0.7 all-gather.2.cloned.1.call-update
  7.9 101.4 %all-gather.2.cloned.1.call-done = bf16[16384,512]{1,0:T(8,128)(2,1)} async-done(((bf16[1024,512]{1,0:T(8,128)(2,1)}), bf16[16384,512]{1,0:T(8,128)(2,1)}) %all-gather.2.cloned.1.call-update) | async-done | bytes 16777232 | tf_op jit(solution)/shard_map/all_gather | solution.py:10
  109.4 13.4 %fusion.34 = f32[256,512]{1,0:T(8,128)} fusion(bf16[256,16384]{1,0:T(8,128)(2,1)} %param.2, bf16[16384,512]{1,0:T(8,128)(2,1)} %all-gather.2.cloned.1.call-done), kind=kOutput, calls=%fused_computation.71 | convolution fusion | flops 4294967296 | bytes 25690112 | tf_op jit(solution)/shard_map/dot_general | solution.py:8
  123.1 91.7 %all-reduce.4.cloned.1.call-done = f32[256,512]{1,0:T(8,128)} async-done(((f32[256,512]{1,0:T(8,128)}), f32[256,512]{1,0:T(8,128)}) %all-reduce.4.cloned.1.call-update) | async-done | bytes 524304 | tf_op jit(solution)/shard_map/psum | solution.py:23
  214.8 3.2 fusion.35
  218.1 113.7 %all-reduce.6.cloned.1.call-done = f32[512,512]{0,1:T(8,128)} async-done(((f32[512,512]{0,1:T(8,128)}), f32[512,512]{0,1:T(8,128)}) %all-reduce.6.cloned.1.call-update) | async-done | bytes 1048592 | tf_op jit(solution)/shard_map/psum | solution.py:24
  331.8 1.3 broadcast_multiply_fusion
  333.5 1.5 fusion
  334.9 11.7 %cholesky.104 = f32[128,128]{1,0:T(8,128)S(1)} custom-call(f32[128,128]{1,0:T(8,128)S(1)} %cholesky.266), custom_call_target="Cholesky" | custom-call | tf_op jit(solution)/shard_map/jit(cholesky)/cholesky | solution.py:27
  346.7 9.8 %custom-call.30 = f32[1,128,128]{1,2,0:T(8,128)S(1)} custom-call(f32[1,128,128]{2,1,0:T(8,128)S(1)} %get-tuple-element.33), custom_call_target="InvertDiagBlocksLowerTriangular" | custom-call | tf_op jit(solution)/shard_map/jit(cholesky)/cholesky | solution.py:27
  357.3 11.8 %cholesky.217 = f32[128,128]{1,0:T(8,128)S(1)} custom-call(f32[128,128]{1,0:T(8,128)S(1)} %cholesky.270), custom_call_target="Cholesky" | custom-call | tf_op jit(solution)/shard_map/jit(cholesky)/cholesky | solution.py:27
  369.2 9.8 %custom-call.31 = f32[1,128,128]{1,2,0:T(8,128)S(1)} custom-call(f32[1,128,128]{2,1,0:T(8,128)S(1)} %get-tuple-element.30), custom_call_target="InvertDiagBlocksLowerTriangular" | custom-call | tf_op jit(solution)/shard_map/jit(cholesky)/cholesky | solution.py:27
  379.7 11.7 %cholesky.238 = f32[128,128]{1,0:T(8,128)S(1)} custom-call(f32[128,128]{1,0:T(8,128)S(1)} %cholesky.275), custom_call_target="Cholesky" | custom-call | tf_op jit(solution)/shard_map/jit(cholesky)/cholesky | solution.py:27
  391.4 0.7 compare_reduce_fusion.1
  392.1 9.8 %custom-call.32 = f32[1,128,128]{1,2,0:T(8,128)S(1)} custom-call(f32[1,128,128]{2,1,0:T(8,128)S(1)} %get-tuple-element.27), custom_call_target="InvertDiagBlocksLowerTriangular" | custom-call | tf_op jit(solution)/shard_map/jit(cholesky)/cholesky | solution.py:27
  402.6 12.0 %cholesky.255 = f32[128,128]{1,0:T(8,128)S(1)} custom-call(f32[128,128]{1,0:T(8,128)S(1)} %convolution_subtract_fusion.2), custom_call_target="Cholesky" | custom-call | tf_op jit(solution)/shard_map/jit(cholesky)/cholesky | solution.py:27
  414.6 0.6 compare_reduce_fusion
  415.2 0.7 compare_reduce_fusion.2
  418.7 1.3 copy.6
  420.0 8.1 %while.1 = (s32[]{:T(128)}, f32[512,512]{1,0:T(8,128)S(1)}, s32[4,2]{0,1:T(2,128)S(1)}, f32[4,128,128]{2,1,0:T(8,128)S(1)}, s32[]{:T(128)}) while((s32[]{:T(128)}, f32[512,512]{1,0:T(8,128)S(1)}, s32[4,2]{0,1:T(2,128)S(1)}, f32[4,128,128]{2,1,0:T(8,128)S(1)}, s32[]{:T(128)}) %tuple.33), condition=%wide.while_cond, body=%wide.while_body.sunk | while | flops 2 | bytes 131181 | solution.py:28
  420.6 1.3 bitcast_dynamic-update-slice_fusion.2
  422.1 0.6 fusion.46
  422.7 1.3 bitcast_dynamic-update-slice_fusion.2
  424.7 1.3 bitcast_dynamic-update-slice_fusion.2
  426.2 0.6 fusion.46
  426.8 1.3 bitcast_dynamic-update-slice_fusion.2
  428.1 39.3 %custom-call.33 = f32[4,128,128]{1,2,0:T(8,128)S(1)} custom-call(f32[4,128,128]{2,1,0:T(8,128)S(1)} %get-tuple-element.9), custom_call_target="InvertDiagBlocksLowerTriangular" | custom-call | tf_op jit(solution)/shard_map/triangular_solve | solution.py:28
  467.4 0.9 fusion.15
  468.3 0.9 convolution_subtract_fusion.5
  469.4 0.9 convolution_subtract_fusion.4
  470.5 1.0 convolution_subtract_fusion.3
  471.7 0.6 pad_maximum_fusion
  (33 shorter events, 5.1 us)
Async XLA Ops:
  7.2 102.2 %all-gather.2.cloned.1.call-start = ((), (), s32[]{:S(2)}) async-start(), calls=%async_computation | async-start | bytes 17825792 | tf_op jit(solution)/shard_map/all_gather | solution.py:10
  7.9 206.9 %all-reduce.4.cloned.1.call-start = ((), (), s32[]{:S(2)}) async-start(), calls=%async_computation.1 | async-start | bytes 1048576 | tf_op jit(solution)/shard_map/psum | solution.py:23
  122.8 209.0 %all-reduce.6.cloned.1.call-start = ((), (), s32[]{:S(2)}) async-start(), calls=%async_computation.2 | async-start | bytes 2097152 | tf_op jit(solution)/shard_map/psum | solution.py:24
Sparse Core Ops, SparseCore 0:
  9.8 99.5 all-gather.1
  123.0 91.8 all-reduce.3
  218.2 113.5 all-reduce.5
where the time goes:
time: 479 us
  waiting for transfers between devices  308 us (64%)
  other arithmetic  122 us (25%)
  matrix products  22.7 us (5%)
  between operations  16.5 us (3%)
  local copies, waits for them, and re-layouts  9.84 us (2%)
    psum x1, waiting for transfers between devices, shards(): gram = lax.psum(gram_term(sketch), 'row')  114 us
    all_gather x1, waiting for transfers between devices, probe_product(): lax.all_gather(test_matrix, 'row', axis=0, tiled=True)  101 us
    psum x1, waiting for transfers between devices, shards(): sketch = lax.psum(partial_value, 'col')  91.7 us
    another operation x14, other arithmetic, shards(): lower_factor = jnp.linalg.cholesky(gram)  78.8 us
    another operation x3, other arithmetic, shards(): lax.linalg.triangular_solve(lower_factor, own_rows, left_side=False, lowe...  40 us
    dot_general x1, matrix products, probe_product(): jnp.dot(matrix, lax.all_gather(test_matrix, 'row', axis=0, tiled=True), p...  13.4 us
  transfers between devices with their start and end apart: 3, of which 3 were waited for; matrix products, arithmetic and copies ran while one was open for 0% of the time, Pallas kernels for 0%

commit v1 on v0

--- a/solution.py
+++ b/solution.py
@@ -1,7 +1,21 @@
+import functools
 import jax
 import jax.numpy as jnp
 from jax import lax
 from jax.sharding import PartitionSpec as P
+
+
+def _render_block(incoming_x, lane_axis):
+    devs = lax.axis_size(lane_axis)
+    piece_out, val = (incoming_x, 0)
+    while 1 << val < devs:
+        val2 = lax.ppermute(piece_out, lane_axis, [(nth, nth ^ 1 << val) for nth in range(devs)])
+        piece_out = piece_out + val2
+        val = val + 1
+    return piece_out
+
+
+groups_treat = functools.partial(_render_block, lane_axis="col")
 
 
 def probe_product(matrix, test_matrix):
@@ -20,7 +34,7 @@
     share_rows = matrix.shape[0] // lax.axis_size("col")
     total_rows = matrix.shape[0] * lax.axis_size("row")
     partial_value = probe_product(matrix, test_matrix)
-    sketch = lax.psum(partial_value, "col")
+    sketch = groups_treat(partial_value)
     gram = lax.psum(gram_term(sketch), "row")
     own_rows = lax.dynamic_slice_in_dim(sketch, lax.axis_index("col") * share_rows, share_rows, 0)
     gram = gram / jnp.float32(total_rows)

time: 479 us -> 440 us (0.919)
  waiting for transfers between devices: 308 us -> 259 us
  starting transfers between devices: 0.3 us -> 8.43 us
    psum x1 -> x0, waiting for transfers between devices: 91.7 us -> none  [shards(): sketch = lax.psum(partial_value, 'col')]
    ppermute x0 -> x4, waiting for transfers between devices: none -> 43 us  [_render_block(): lax.ppermute(piece_out, lane_axis, [(nth, nth ^ 1 << val) for nth in rang...]
    ppermute x0 -> x4, starting transfers between devices: none -> 8.35 us  [_render_block(): lax.ppermute(piece_out, lane_axis, [(nth, nth ^ 1 << val) for nth in rang...]
  transfers between devices with their start and end apart: 3 -> 6, of which waited for: 3 -> 6; matrix products, arithmetic and copies ran while one was open for 0% -> 0% of each run, Pallas kernels for 0% -> 0%
where the time goes in v1:
time: 440 us; the launch traced here: 439 us
  waiting for transfers between devices  259 us (59%)
  other arithmetic  123 us (28%)
  matrix products  18.5 us (4%)
  between operations  16.8 us (4%)
  local copies, waits for them, and re-layouts  13.4 us (3%)
  starting transfers between devices  8.43 us (2%)
    psum x1, waiting for transfers between devices, shards(): gram = lax.psum(gram_term(sketch), 'row')  114 us
    all_gather x1, waiting for transfers between devices, probe_product(): lax.all_gather(test_matrix, 'row', axis=0, tiled=True)  101 us
    another operation x14, other arithmetic, shards(): lower_factor = jnp.linalg.cholesky(gram)  78.8 us
    ppermute x4, waiting for transfers between devices, _render_block(): lax.ppermute(piece_out, lane_axis, [(nth, nth ^ 1 << val) for nth in rang...  43 us
    another operation x3, other arithmetic, shards(): lax.linalg.triangular_solve(lower_factor, own_rows, left_side=False, lowe...  40 us
    another operation x12, local copies, waits for them, and re-layouts  11.6 us
    dot_general x1, matrix products, probe_product(): jnp.dot(matrix, lax.all_gather(test_matrix, 'row', axis=0, tiled=True), p...  10.5 us
  transfers between devices with their start and end apart: 6, of which 6 were waited for; matrix products, arithmetic and copies ran while one was open for 0% of the time, Pallas kernels for 0%

profile of v1, /device:TPU:1, one launch (start us, length us, event | category | flops | bytes accessed | tf_op | source)
XLA Modules:
  0.0 439.1 jit_solution(10984597754903419416)
XLA Ops:
  7.9 101.4 %all-gather.2.cloned.1.call-done = bf16[16384,512]{1,0:T(8,128)(2,1)} async-done(((bf16[1024,512]{1,0:T(8,128)(2,1)}), bf16[16384,512]{1,0:T(8,128)(2,1)}) %all-gather.2.cloned.1.call-update) | async-done | bytes 16777232 | tf_op jit(solution)/shard_map/all_gather | solution.py:24
  109.4 10.5 %fusion.37 = f32[256,512]{1,0:T(8,128)S(1)} fusion(bf16[256,16384]{1,0:T(8,128)(2,1)} %param.2, bf16[16384,512]{1,0:T(8,128)(2,1)} %all-gather.2.cloned.1.call-done), kind=kOutput, calls=%fused_computation.74 | convolution fusion | flops 4294967296 | bytes 25690112 | tf_op jit(solution)/shard_map/dot_general | solution.py:22
  119.9 1.3 collective-permute-start
  121.2 12.0 %collective-permute-done = f32[256,512]{1,0:T(8,128)S(1)} collective-permute-done((f32[256,512]{1,0:T(8,128)S(1)}, f32[256,512]{1,0:T(8,128)S(1)}, u32[]{:S(2)}, u32[]{:S(2)}) %collective-permute-start) | collective-permute-done | bytes 524320 | tf_op jit(solution)/shard_map/ppermute | solution.py:12
  133.3 2.8 collective-permute-start.1
  136.1 11.2 %collective-permute-done.1 = f32[256,512]{1,0:T(8,128)S(1)} collective-permute-done((f32[256,512]{1,0:T(8,128)S(1)}, f32[256,512]{1,0:T(8,128)S(1)}, u32[]{:S(2)}, u32[]{:S(2)}) %collective-permute-start.1) | collective-permute-done | bytes 524320 | tf_op jit(solution)/shard_map/ppermute | solution.py:12
  147.3 1.3 collective-permute-start.2
  148.6 10.3 %collective-permute-done.2 = f32[256,512]{1,0:T(8,128)S(1)} collective-permute-done((f32[256,512]{1,0:T(8,128)S(1)}, f32[256,512]{1,0:T(8,128)S(1)}, u32[]{:S(2)}, u32[]{:S(2)}) %collective-permute-start.2) | collective-permute-done | bytes 524320 | tf_op jit(solution)/shard_map/ppermute | solution.py:12
  159.0 3.0 collective-permute-start.3
  162.0 9.5 %collective-permute-done.3 = f32[256,512]{1,0:T(8,128)S(1)} collective-permute-done((f32[256,512]{1,0:T(8,128)S(1)}, f32[256,512]{1,0:T(8,128)S(1)}, u32[]{:S(2)}, u32[]{:S(2)}) %collective-permute-start.3) | collective-permute-done | bytes 524320 | tf_op jit(solution)/shard_map/ppermute | solution.py:12
  171.6 2.0 fusion.38
  173.7 113.7 %all-reduce.3.cloned.1.call-done = f32[512,512]{0,1:T(8,128)} async-done(((f32[512,512]{0,1:T(8,128)}), f32[512,512]{0,1:T(8,128)}) %all-reduce.3.cloned.1.call-update) | async-done | bytes 1048592 | tf_op jit(solution)/shard_map/psum | solution.py:38
  287.4 1.3 broadcast_multiply_fusion
  289.0 1.5 fusion
  290.5 11.7 %cholesky.104 = f32[128,128]{1,0:T(8,128)S(1)} custom-call(f32[128,128]{1,0:T(8,128)S(1)} %cholesky.266), custom_call_target="Cholesky" | custom-call | tf_op jit(solution)/shard_map/jit(cholesky)/cholesky | solution.py:41
  302.3 9.8 %custom-call.30 = f32[1,128,128]{1,2,0:T(8,128)S(1)} custom-call(f32[1,128,128]{2,1,0:T(8,128)S(1)} %get-tuple-element.33), custom_call_target="InvertDiagBlocksLowerTriangular" | custom-call | tf_op jit(solution)/shard_map/jit(cholesky)/cholesky | solution.py:41
  312.9 11.9 %cholesky.217 = f32[128,128]{1,0:T(8,128)S(1)} custom-call(f32[128,128]{1,0:T(8,128)S(1)} %cholesky.270), custom_call_target="Cholesky" | custom-call | tf_op jit(solution)/shard_map/jit(cholesky)/cholesky | solution.py:41
  324.8 9.8 %custom-call.31 = f32[1,128,128]{1,2,0:T(8,128)S(1)} custom-call(f32[1,128,128]{2,1,0:T(8,128)S(1)} %get-tuple-element.30), custom_call_target="InvertDiagBlocksLowerTriangular" | custom-call | tf_op jit(solution)/shard_map/jit(cholesky)/cholesky | solution.py:41
  335.2 11.7 %cholesky.238 = f32[128,128]{1,0:T(8,128)S(1)} custom-call(f32[128,128]{1,0:T(8,128)S(1)} %cholesky.275), custom_call_target="Cholesky" | custom-call | tf_op jit(solution)/shard_map/jit(cholesky)/cholesky | solution.py:41
  347.7 9.8 %custom-call.32 = f32[1,128,128]{1,2,0:T(8,128)S(1)} custom-call(f32[1,128,128]{2,1,0:T(8,128)S(1)} %get-tuple-element.27), custom_call_target="InvertDiagBlocksLowerTriangular" | custom-call | tf_op jit(solution)/shard_map/jit(cholesky)/cholesky | solution.py:41
  358.1 11.9 %cholesky.255 = f32[128,128]{1,0:T(8,128)S(1)} custom-call(f32[128,128]{1,0:T(8,128)S(1)} %convolution_subtract_fusion.2), custom_call_target="Cholesky" | custom-call | tf_op jit(solution)/shard_map/jit(cholesky)/cholesky | solution.py:41
  373.9 1.3 fusion.2
  375.2 1.3 copy.6
  376.5 11.7 %while.1 = (s32[]{:T(128)}, f32[512,512]{1,0:T(8,128)}, s32[4,2]{0,1:T(2,128)S(1)}, f32[4,128,128]{2,1,0:T(8,128)S(1)}, s32[]{:T(128)}) while((s32[]{:T(128)}, f32[512,512]{1,0:T(8,128)}, s32[4,2]{0,1:T(2,128)S(1)}, f32[4,128,128]{2,1,0:T(8,128)S(1)}, s32[]{:T(128)}) %tuple.33), condition=%wide.while_cond, body=%wide.while_body.sunk | while | flops 2 | bytes 131181 | solution.py:42
  377.2 2.3 bitcast_dynamic-update-slice_fusion.2
  380.1 2.3 bitcast_dynamic-update-slice_fusion.2
  383.1 2.3 bitcast_dynamic-update-slice_fusion.2
  386.0 2.2 bitcast_dynamic-update-slice_fusion.2
  388.2 39.3 %custom-call.33 = f32[4,128,128]{1,2,0:T(8,128)S(1)} custom-call(f32[4,128,128]{2,1,0:T(8,128)S(1)} %get-tuple-element.9), custom_call_target="InvertDiagBlocksLowerTriangular" | custom-call | tf_op jit(solution)/shard_map/triangular_solve | solution.py:42
  427.7 1.0 fusion.16
  428.9 1.1 fusion.9
  430.2 1.3 fusion.4
  (42 shorter events, 9.7 us)
Async XLA Ops:
  7.2 102.2 %all-gather.2.cloned.1.call-start = ((), (), s32[]{:S(2)}) async-start(), calls=%async_computation | async-start | bytes 17825792 | tf_op jit(solution)/shard_map/all_gather | solution.py:24
  7.9 279.5 %all-reduce.3.cloned.1.call-start = ((), (), s32[]{:S(2)}) async-start(), calls=%async_computation.1 | async-start | bytes 2097152 | tf_op jit(solution)/shard_map/psum | solution.py:38
  119.9 13.3 %collective-permute-start = (f32[256,512]{1,0:T(8,128)S(1)}, f32[256,512]{1,0:T(8,128)S(1)}, u32[]{:S(2)}, u32[]{:S(2)}) collective-permute-start(f32[256,512]{1,0:T(8,128)S(1)} %fusion.37), channel_id=1, source_target_pairs={{0,1},{1,0},{2,3},{3,2},{4,5},{5,4},{6,7},{7,6},{8,9},{9,8},{10,11... | collective-permute-start | bytes 1572872 | tf_op jit(solution)/shard_map/ppermute | solution.py:12
  133.3 14.0 %collective-permute-start.1 = (f32[256,512]{1,0:T(8,128)S(1)}, f32[256,512]{1,0:T(8,128)S(1)}, u32[]{:S(2)}, u32[]{:S(2)}) collective-permute-start(f32[256,512]{1,0:T(8,128)S(1)} %add.57), channel_id=1, source_target_pairs={{0,2},{1,3},{2,0},{3,1},{4,6},{5,7},{6,4},{7,5},{8,10},{9,11},{10,... | collective-permute-start | bytes 1572872 | tf_op jit(solution)/shard_map/ppermute | solution.py:12
  147.3 11.6 %collective-permute-start.2 = (f32[256,512]{1,0:T(8,128)S(1)}, f32[256,512]{1,0:T(8,128)S(1)}, u32[]{:S(2)}, u32[]{:S(2)}) collective-permute-start(f32[256,512]{1,0:T(8,128)S(1)} %add.58), channel_id=1, source_target_pairs={{0,4},{1,5},{2,6},{3,7},{4,0},{5,1},{6,2},{7,3},{8,12},{9,13},{10,... | collective-permute-start | bytes 1572872 | tf_op jit(solution)/shard_map/ppermute | solution.py:12
  159.0 12.5 %collective-permute-start.3 = (f32[256,512]{1,0:T(8,128)S(1)}, f32[256,512]{1,0:T(8,128)S(1)}, u32[]{:S(2)}, u32[]{:S(2)}) collective-permute-start(f32[256,512]{1,0:T(8,128)S(1)} %add.59), channel_id=1, source_target_pairs={{0,8},{1,9},{2,10},{3,11},{4,12},{5,13},{6,14},{7,15},{8,0},{9,1},... | collective-permute-start | bytes 1572872 | tf_op jit(solution)/shard_map/ppermute | solution.py:12
Sparse Core Ops, SparseCore 0:
  9.8 99.5 all-gather.1
  173.8 113.5 all-reduce.2
